TPU v7x, 256 devices: a whole 4x4x8 slice. The times are simulated.
256 devices in a mesh: seq: 32 (over y, z_hi, core), head: 8 (over z_lo, x).
Axes of the slice: x: 4, y: 4, z: 8 (z_hi: 4, z_lo: 2; z = z_hi * 2 + z_lo), core: 2. Of those that a mesh axis runs over, the one named last changes fastest.
Arguments:
- xin: bfloat16 [16384, 8192], P('seq', 'head'), may hold values from -6 to 6
- gate_z: bfloat16 [16384, 8192], P('seq', 'head'), may hold values from -6 to 6
- b_proj: bfloat16 [16384, 8, 256], P('seq', 'head'), may hold values from -0.375 to 0.375
- c_proj: bfloat16 [16384, 8, 256], P('seq', 'head'), may hold values from -0.375 to 0.375
- log_retain: float32 [16384, 128], P('seq', 'head'), may hold values from -2 to 0, as said below
- skip_d: float32 [128], P('head'), may hold values from 0.5 to 2
- norm_gain: float32 [8192], P('head'), may hold values from 0.5 to 1.5
- w_out: bfloat16 [8192, 4096], P('head', 'seq'), may hold values from -0.0625 to 0.0625
- residual: bfloat16 [16384, 4096], P(('seq', 'head')), may hold values from -24 to 24
- refusal: float32 [4096], replicated, may hold values from -6 to 6
- stream_gain: float32 [4096], replicated, may hold values from 0.5 to 1.5
- w_in: bfloat16 [4096, 8192], P('seq', 'head'), may hold values from -0.09375 to 0.09375
Outputs:
- stream: bfloat16 [16384, 4096], P(('seq', 'head'))
- next_x: bfloat16 [16384, 8192], P('seq', 'head')
Inputs may be any that keep to these rules, and one draw needn't show every extreme that they name: `log_retain`: every entry is negative.
All inputs are finite; a program needn't handle non-finite values.
Results may differ from a plain program's by a relative error of at most 0.02.
Values may be sent and summed in bfloat16 or wider, within the bound.
No kernel may reach another device: no remote copies, remote signals or barrier semaphores. Data moves between devices by JAX's collectives and lax.ppermute only.
A program may use at most 192 MiB of HBM per device.

v0:
```python
import jax
import jax.numpy as jnp
from jax import lax
from jax.sharding import PartitionSpec as P

SPAN = 256


def shift_scan(decay, state, axis):
    devices = lax.axis_size(axis)

    def shifted(parts, distance):
        pairs = [(i, i + distance) for i in range(devices - distance)]
        a, s = parts
        return (
            lax.ppermute(a, axis, pairs),
            lax.ppermute(s.astype(jnp.bfloat16), axis, pairs).astype(jnp.float32),
        )

    acc = shifted((decay, state), 1)
    distance = 1
    while distance < devices:
        acc = carry_combine(shifted(acc, distance), acc)
        distance *= 2
    return acc


def carry_combine(earlier, later):
    decay_early, state_early = earlier
    decay_later, state_later = later
    return (
        decay_early + decay_later,
        jnp.exp(decay_later).reshape((-1,) + (1,) * (state_later.ndim - 1)) * state_early
        + state_later,
    )


def body(
    xin,
    gate_z,
    b_proj,
    c_proj,
    log_retain,
    skip_d,
    norm_gain,
    w_out,
    residual,
    refusal,
    stream_gain,
    w_in,
):
    seq_rows, channels = xin.shape
    head_count = log_retain.shape[1]
    head_width = channels // head_count
    group_count = b_proj.shape[1]
    state_width = b_proj.shape[2]
    per_group = head_count // group_count
    block_count = seq_rows // SPAN
    inputs = xin.reshape(block_count, SPAN, head_count, head_width)
    b_grouped = b_proj.reshape(block_count, SPAN, group_count, state_width)
    c_grouped = c_proj.reshape(block_count, SPAN, group_count, state_width)
    scores = jnp.einsum("klgn,ksgn->kgls", c_grouped, b_grouped, preferred_element_type=jnp.float32)
    scores = jnp.repeat(scores, per_group, axis=1)
    cum = jnp.cumsum(log_retain.reshape(block_count, SPAN, head_count), axis=1)
    cum_heads = jnp.transpose(cum, (0, 2, 1))
    later_pos = lax.broadcasted_iota(jnp.int32, (SPAN, SPAN), 0)
    earlier_pos = lax.broadcasted_iota(jnp.int32, (SPAN, SPAN), 1)
    causal = later_pos >= earlier_pos
    gap = cum_heads[:, :, :, None] - cum_heads[:, :, None, :]
    mixing = (jnp.where(causal, jnp.exp(jnp.where(causal, gap, 0.0)), 0.0) * scores).astype(
        jnp.bfloat16
    )
    intra = jnp.einsum("khls,kshp->klhp", mixing, inputs, preferred_element_type=jnp.float32)
    tail_decay = jnp.exp(cum_heads[:, :, -1:] - cum_heads)
    b_heads = jnp.repeat(b_grouped, per_group, axis=2)
    weighted_b = (
        b_heads.astype(jnp.float32) * jnp.transpose(tail_decay, (0, 2, 1))[..., None]
    ).astype(jnp.bfloat16)
    block_state = jnp.einsum(
        "klhn,klhp->khnp", weighted_b, inputs, preferred_element_type=jnp.float32
    )
    block_decay = cum_heads[:, :, -1]
    device_state = jnp.zeros((head_count, state_width, head_width), jnp.float32)
    starts_list = []
    for block in range(block_count):
        starts_list.append(device_state)
        device_state = (
            jnp.exp(block_decay[block])[:, None, None] * device_state + block_state[block]
        )
    local_starts = jnp.stack(starts_list)
    device_decay = jnp.sum(block_decay, axis=0)
    total_decay, incoming = shift_scan(
        device_decay, device_state.reshape(head_count, state_width * head_width), "seq"
    )
    incoming = incoming.reshape(head_count, state_width, head_width)
    before_block = jnp.cumsum(block_decay, axis=0) - block_decay
    starts = local_starts + jnp.exp(before_block)[:, :, None, None] * incoming[None]
    c_heads = jnp.repeat(c_grouped, per_group, axis=2).astype(jnp.float32)
    carried = jnp.einsum("klhn,khnp->klhp", c_heads, starts, precision=lax.Precision.HIGHEST)
    carried = carried * jnp.exp(cum)[..., None]
    mixed = intra + carried + skip_d[None, None, :, None] * inputs.astype(jnp.float32)
    gated = mixed * jax.nn.silu(
        gate_z.reshape(block_count, SPAN, head_count, head_width).astype(jnp.float32)
    )
    grouped = gated.reshape(seq_rows, group_count, per_group * head_width)
    grouped = grouped * lax.rsqrt(jnp.mean(grouped * grouped, axis=-1, keepdims=True) + 1e-05)
    ssd_out = (grouped.reshape(seq_rows, channels) * norm_gain[None, :]).astype(jnp.bfloat16)
    w_in_all = lax.all_gather(w_in, "seq", axis=0, tiled=True)
    ssd_out, w_in_all = lax.optimization_barrier((ssd_out, w_in_all))
    own_rows = residual.shape[0]
    mine = lax.axis_index("head")
    head_devices = seq_rows // own_rows
    in_block = lax.broadcasted_iota(jnp.int32, (head_devices, 1, 1), 0) == mine
    residual_rows = jnp.where(in_block, residual.astype(jnp.float32)[None], 0.0).reshape(
        seq_rows, residual.shape[1]
    )
    partial_sum = jnp.dot(
        ssd_out,
        lax.all_gather(w_out, "seq", axis=1, tiled=True),
        preferred_element_type=jnp.float32,
    )
    with_residual = (partial_sum + residual_rows).astype(jnp.bfloat16)
    hidden = lax.psum(with_residual, "head").astype(jnp.float32)
    unit = refusal / jnp.sqrt(jnp.sum(refusal * refusal) + 1e-06)
    coef = jnp.dot(hidden, unit, precision=lax.Precision.HIGH)
    stream_all = (hidden - coef[:, None] * unit[None, :]).astype(jnp.bfloat16)
    stream_float = stream_all.astype(jnp.float32)
    all_rows = (
        stream_float
        * lax.rsqrt(jnp.mean(stream_float * stream_float, axis=-1, keepdims=True) + 1e-05)
        * stream_gain[None, :]
    ).astype(jnp.bfloat16)
    stream = lax.dynamic_slice_in_dim(stream_all, mine * own_rows, own_rows)
    next_float = jnp.dot(all_rows, w_in_all, preferred_element_type=jnp.float32)
    return (stream, next_float.astype(jnp.bfloat16))


def solution(mesh):
    in_specs = (
        P("seq", "head"),
        P("seq", "head"),
        P("seq", "head", None),
        P("seq", "head", None),
        P("seq", "head"),
        P("head"),
        P("head"),
        P("head", "seq"),
        P(("seq", "head"), None),
        P(),
        P(),
        P("seq", "head"),
    )
    out_specs = (P(("seq", "head"), None), P("seq", "head"))
    return jax.shard_map(body, mesh=mesh, in_specs=in_specs, out_specs=out_specs, check_vma=False)
```

profile of v0, /device:TPU:1, one launch (start us, length us, event | category | flops | bytes accessed | tf_op | source)
XLA Modules:
  0.0 363.6 jit_solution(14837152535283461224)
XLA Ops:
  7.2 0.7 all-gather.3.cloned.1.call-update
  8.0 0.8 copy_bitcast_fusion.1
  8.7 1.1 reduce-window.6
  10.1 3.0 reshape.187
  13.0 1.7 copy.36
  14.7 1.2 convert_element_type.79
  16.4 0.7 exponential_bitcast_fusion
  17.1 1.6 fusion.6
  18.7 1.6 fusion.43
  21.6 1.8 copy.38
  23.4 1.7 squeeze.4
  25.1 1.4 add_convert_fusion
  26.6 6.3 %collective-permute-start.5 = (bf16[16,16384]{1,0:T(8,128)(2,1)S(1)}, bf16[16,16384]{1,0:T(8,128)(2,1)S(1)}, u32[]{:S(2)}, u32[]{:S(2)}) collective-permute-start(bf16[16,16384]{1,0:T(8,128)(2,1)S(1)} %add_convert_fusion), channel_id=1, source_target_pairs={{0,8},{8,16},{16,24},{24,32},{32,40},{40,48},{48,56},{56,64},{64,7... | collective-permute-start | bytes 1572872 | tf_op jit(solution)/shard_map/ppermute | solution.py:17
  32.9 15.5 %collective-permute-done.5 = bf16[16,16384]{1,0:T(8,128)(2,1)S(1)} collective-permute-done((bf16[16,16384]{1,0:T(8,128)(2,1)S(1)}, bf16[16,16384]{1,0:T(8,128)(2,1)S(1)}, u32[]{:S(2)}, u32[]{:S(2)}) %collective-permute-start.5) | collective-permute-done | bytes 524320 | tf_op jit(solution)/shard_map/ppermute | solution.py:17
  48.4 6.1 %collective-permute-start.6 = (bf16[16,16384]{1,0:T(8,128)(2,1)S(1)}, bf16[16,16384]{1,0:T(8,128)(2,1)S(1)}, u32[]{:S(2)}, u32[]{:S(2)}) collective-permute-start(bf16[16,16384]{1,0:T(8,128)(2,1)S(1)} %collective-permute-done.5), channel_id=1, source_target_pairs={{0,8},{8,16},{16,24},{24,32},{32,40},{40,48},{48,56},{56,64},{64,7... | collective-permute-start | bytes 1572872 | tf_op jit(solution)/shard_map/ppermute | solution.py:17
  54.5 2.5 collective-permute-start
  57.1 20.6 %collective-permute-done = f32[16]{0:T(128)S(1)} collective-permute-done((f32[16]{0:T(128)S(1)}, f32[16]{0:T(128)S(1)}, u32[]{:S(2)}, u32[]{:S(2)}) %collective-permute-start) | collective-permute-done | bytes 96 | tf_op jit(solution)/shard_map/ppermute | solution.py:16
  77.7 5.7 %collective-permute-start.1 = (f32[16]{0:T(128)S(1)}, f32[16]{0:T(128)S(1)}, u32[]{:S(2)}, u32[]{:S(2)}) collective-permute-start(f32[16]{0:T(128)S(1)} %collective-permute-done), channel_id=1, source_target_pairs={{0,8},{8,16},{16,24},{24,32},{32,40},{40,48},{48,56},{56,64},{64,7... | collective-permute-start | bytes 200 | tf_op jit(solution)/shard_map/ppermute | solution.py:16
  83.4 0.7 collective-permute-done.1
  84.3 23.8 %collective-permute-start.7 = (bf16[16,16384]{1,0:T(8,128)(2,1)S(1)}, bf16[16,16384]{1,0:T(8,128)(2,1)S(1)}, u32[]{:S(2)}, u32[]{:S(2)}) collective-permute-start(bf16[16,16384]{1,0:T(8,128)(2,1)S(1)} %fusion.31), channel_id=1, source_target_pairs={{0,16},{8,24},{16,32},{24,40},{32,48},{40,56},{48,64},{56,72},{64,... | collective-permute-start | bytes 1572872 | tf_op jit(solution)/shard_map/ppermute | solution.py:17
  108.2 13.9 %collective-permute-done.7 = bf16[16,16384]{1,0:T(8,128)(2,1)S(1)} collective-permute-done((bf16[16,16384]{1,0:T(8,128)(2,1)S(1)}, bf16[16,16384]{1,0:T(8,128)(2,1)S(1)}, u32[]{:S(2)}, u32[]{:S(2)}) %collective-permute-start.7) | collective-permute-done | bytes 524320 | tf_op jit(solution)/shard_map/ppermute | solution.py:17
  122.5 10.4 %collective-permute-start.8 = (bf16[16,16384]{1,0:T(8,128)(2,1)S(1)}, bf16[16,16384]{1,0:T(8,128)(2,1)S(1)}, u32[]{:S(2)}, u32[]{:S(2)}) collective-permute-start(bf16[16,16384]{1,0:T(8,128)(2,1)S(1)} %fusion.39), channel_id=1, source_target_pairs={{0,32},{8,40},{16,48},{24,56},{32,64},{40,72},{48,80},{56,88},{64,... | collective-permute-start | bytes 1572872 | tf_op jit(solution)/shard_map/ppermute | solution.py:17
  133.0 2.1 collective-permute-start.2
  135.0 24.5 %collective-permute-done.2 = f32[16]{0:T(128)S(1)} collective-permute-done((f32[16]{0:T(128)S(1)}, f32[16]{0:T(128)S(1)}, u32[]{:S(2)}, u32[]{:S(2)}) %collective-permute-start.2) | collective-permute-done | bytes 96 | tf_op jit(solution)/shard_map/ppermute | solution.py:16
  160.0 1.5 collective-permute-start.9
  161.5 8.3 %collective-permute-start.3 = (f32[16]{0:T(128)S(1)}, f32[16]{0:T(128)S(1)}, u32[]{:S(2)}, u32[]{:S(2)}) collective-permute-start(f32[16]{0:T(128)S(1)} %get-tuple-element.15), channel_id=1, source_target_pairs={{0,32},{8,40},{16,48},{24,56},{32,64},{40,72},{48,80},{56,88},{64,... | collective-permute-start | bytes 200 | tf_op jit(solution)/shard_map/ppermute | solution.py:16
  169.8 0.7 collective-permute-done.3
  170.5 1.3 fusion.38
  171.9 15.1 %collective-permute-start.10 = (bf16[16,16384]{1,0:T(8,128)(2,1)}, bf16[16,16384]{1,0:T(8,128)(2,1)}, u32[]{:S(2)}, u32[]{:S(2)}) collective-permute-start(bf16[16,16384]{1,0:T(8,128)(2,1)} %fusion.38), channel_id=1, source_target_pairs={{0,128},{8,136},{16,144},{24,152},{32,160},{40,168},{48,176},{56,1... | collective-permute-start | bytes 1572872 | tf_op jit(solution)/shard_map/ppermute | solution.py:17
  186.9 4.1 %reshape.188 = f32[2,256,16,64]{3,2,1,0:T(8,128)} reshape(bf16[512,1024]{1,0:T(8,128)(2,1)} %param.13) | data formatting | bytes 3145728 | tf_op jit(solution)/shard_map/convert_element_type | solution.py:103
  191.0 4.6 %copy.44 = f32[2,256,16,64]{1,3,2,0:T(8,128)} copy(f32[2,256,16,64]{3,2,1,0:T(8,128)} %reshape.188) | data formatting | bytes 4194304 | tf_op jit(solution)/shard_map/convert_element_type | solution.py:103
  195.8 1.1 fusion.44
  196.9 1.5 collective-permute-start.4
  198.3 2.1 convert_element_type.96
  200.9 2.7 multiply_add_fusion
  203.6 2.1 mul.195
  206.3 5.3 %fusion.21 = f32[2,16,64,256]{3,2,1,0:T(8,128)S(1)} fusion(bf16[2,256,256]{2,1,0:T(8,128)(2,1)S(1)} %bitcast.66, f32[1,16,256,64]{2,3,1,0:T(8,128)} %get-tuple-element.19, f32[16,256,64]{1,2,0:T(8,128)S(1)} %copy.40, f32[2,16]{1,0:T(2,128)S(1)} %subtract_exponential_fusion), kind=kOutput, calls=%fused_computation.29 | convolution fusion | flops 1611661312 | bytes 4456576 | tf_op jit(solution)/shard_map/klhn,khnp->klhp/dot_general | solution.py:99
  211.7 3.1 multiply_reduce_fusion
  214.8 1.6 copy.45
  216.9 8.2 %all-gather.5.cloned.1.call-done = bf16[1024,4096]{1,0:T(8,128)(2,1)} async-done(((bf16[1024,128]{1,0:T(8,128)(2,1)}), bf16[1024,4096]{1,0:T(8,128)(2,1)}) %all-gather.5.cloned.1.call-update) | async-done | bytes 8388624 | tf_op jit(solution)/shard_map/all_gather | solution.py:119
  225.2 9.7 %fusion.4 = bf16[512,4096]{1,0:T(8,128)(2,1)} fusion(bf16[512,1024]{0,1:T(8,128)(2,1)S(1)} %multiply_convert_fusion.4, bf16[1024,4096]{1,0:T(8,128)(2,1)} %all-gather.5.cloned.1.call-done, f32[64,4096]{1,0:T(8,128)S(1)} %copy-done.6, pred[512]{0:T(512)(128)(4,1)S(1)} %broadcast_in_dim.63), kind=kOutput, calls=%fused_computation.7 | convolution fusion | flops 4301258752 | bytes 14680576 | tf_op jit(solution)/shard_map/dot_general | solution.py:117
  234.9 0.7 copy-done.9
  236.9 106.3 %all-reduce.3.cloned.1.call-done = bf16[512,4096]{1,0:T(8,128)(2,1)} async-done(((bf16[512,4096]{1,0:T(8,128)(2,1)}), bf16[512,4096]{1,0:T(8,128)(2,1)}) %all-reduce.3.cloned.1.call-update) | async-done | bytes 4194320 | tf_op jit(solution)/shard_map/psum | solution.py:123
  343.3 4.6 %fusion.45 = f32[1,512]{1,0:T(1,128)S(1)} fusion(bf16[512,4096]{1,0:T(8,128)(2,1)} %all-reduce.3.cloned.1.call-done, f32[4096,1]{0,1:T(1,128)S(1)} %bitcast.71), kind=kOutput, calls=%fused_computation.78 | convolution fusion | flops 12582912 | bytes 4212736 | tf_op jit(solution)/shard_map/dot_general | solution.py:125
  347.9 1.9 fusion
  349.8 0.8 constant_dynamic-slice_fusion
  350.7 0.8 copy-done.12
  351.5 5.6 %fusion.26 = bf16[512,1024]{1,0:T(8,128)(2,1)} fusion(bf16[4096,1024]{1,0:T(8,128)(2,1)S(1)} %copy-done.12, bf16[512,4096]{1,0:T(8,128)(2,1)S(1)} %get-tuple-element.11, f32[4096]{0:T(1024)S(1)} %copy-done.13, f32[512]{0:T(512)S(1)} %add_rsqrt_fusion), kind=kOutput, calls=%fused_computation.34 | convolution fusion | flops 4303880192 | bytes 13649920 | tf_op jit(solution)/shard_map/dot_general | solution.py:134
  (68 shorter events, 5.6 us)
Async XLA Ops:
  7.2 188.6 %copy-start = (bf16[512,1,256]{2,0,1:T(8,128)(2,1)S(1)}, bf16[512,1,256]{2,0,1:T(8,128)(2,1)}, u32[]{:S(2)}) copy-start(bf16[512,1,256]{2,0,1:T(8,128)(2,1)} %param.15) | copy-start | bytes 786436
  7.2 209.7 %all-gather.3.cloned.1.call-start = ((), (), s32[]{:S(2)}) async-start(), calls=%async_computation | async-start | bytes 8650752 | tf_op jit(solution)/shard_map/all_gather | solution.py:108
  7.9 217.2 %all-gather.5.cloned.1.call-start = ((), (), s32[]{:S(2)}) async-start(), calls=%async_computation.1 | async-start | bytes 8650752 | tf_op jit(solution)/shard_map/all_gather | solution.py:119
  14.7 5.6 %copy-start.4 = (bf16[2,256,16,64]{1,3,2,0:T(8,128)(2,1)}, bf16[2,256,16,64]{1,3,2,0:T(8,128)(2,1)S(1)}, u32[]{:S(2)}) copy-start(bf16[2,256,16,64]{1,3,2,0:T(8,128)(2,1)S(1)} %copy.36) | copy-start | bytes 3145732
  26.6 21.8 %collective-permute-start.5 = (bf16[16,16384]{1,0:T(8,128)(2,1)S(1)}, bf16[16,16384]{1,0:T(8,128)(2,1)S(1)}, u32[]{:S(2)}, u32[]{:S(2)}) collective-permute-start(bf16[16,16384]{1,0:T(8,128)(2,1)S(1)} %add_convert_fusion), channel_id=1, source_target_pairs={{0,8},{8,16},{16,24},{24,32},{32,40},{40,48},{48,56},{56,64},{64,7... | collective-permute-start | bytes 1572872 | tf_op jit(solution)/shard_map/ppermute | solution.py:17
  48.4 35.7 %collective-permute-start.6 = (bf16[16,16384]{1,0:T(8,128)(2,1)S(1)}, bf16[16,16384]{1,0:T(8,128)(2,1)S(1)}, u32[]{:S(2)}, u32[]{:S(2)}) collective-permute-start(bf16[16,16384]{1,0:T(8,128)(2,1)S(1)} %collective-permute-done.5), channel_id=1, source_target_pairs={{0,8},{8,16},{16,24},{24,32},{32,40},{40,48},{48,56},{56,64},{64,7... | collective-permute-start | bytes 1572872 | tf_op jit(solution)/shard_map/ppermute | solution.py:17
  54.5 23.2 %collective-permute-start = (f32[16]{0:T(128)S(1)}, f32[16]{0:T(128)S(1)}, u32[]{:S(2)}, u32[]{:S(2)}) collective-permute-start(f32[16]{0:T(128)S(1)} %get-tuple-element.6), channel_id=1, source_target_pairs={{0,8},{8,16},{16,24},{24,32},{32,40},{40,48},{48,56},{56,64},{64,7... | collective-permute-start | bytes 200 | tf_op jit(solution)/shard_map/ppermute | solution.py:16
  77.7 6.4 %collective-permute-start.1 = (f32[16]{0:T(128)S(1)}, f32[16]{0:T(128)S(1)}, u32[]{:S(2)}, u32[]{:S(2)}) collective-permute-start(f32[16]{0:T(128)S(1)} %collective-permute-done), channel_id=1, source_target_pairs={{0,8},{8,16},{16,24},{24,32},{32,40},{40,48},{48,56},{56,64},{64,7... | collective-permute-start | bytes 200 | tf_op jit(solution)/shard_map/ppermute | solution.py:16
  84.3 37.8 %collective-permute-start.7 = (bf16[16,16384]{1,0:T(8,128)(2,1)S(1)}, bf16[16,16384]{1,0:T(8,128)(2,1)S(1)}, u32[]{:S(2)}, u32[]{:S(2)}) collective-permute-start(bf16[16,16384]{1,0:T(8,128)(2,1)S(1)} %fusion.31), channel_id=1, source_target_pairs={{0,16},{8,24},{16,32},{24,40},{32,48},{40,56},{48,64},{56,72},{64,... | collective-permute-start | bytes 1572872 | tf_op jit(solution)/shard_map/ppermute | solution.py:17
  108.2 235.1 %all-reduce.3.cloned.1.call-start = ((), (), s32[]{:S(2)}) async-start(), calls=%async_computation.2 | async-start | bytes 8388608 | tf_op jit(solution)/shard_map/psum | solution.py:123
  122.5 37.0 %collective-permute-start.8 = (bf16[16,16384]{1,0:T(8,128)(2,1)S(1)}, bf16[16,16384]{1,0:T(8,128)(2,1)S(1)}, u32[]{:S(2)}, u32[]{:S(2)}) collective-permute-start(bf16[16,16384]{1,0:T(8,128)(2,1)S(1)} %fusion.39), channel_id=1, source_target_pairs={{0,32},{8,40},{16,48},{24,56},{32,64},{40,72},{48,80},{56,88},{64,... | collective-permute-start | bytes 1572872 | tf_op jit(solution)/shard_map/ppermute | solution.py:17
  133.0 26.5 %collective-permute-start.2 = (f32[16]{0:T(128)S(1)}, f32[16]{0:T(128)S(1)}, u32[]{:S(2)}, u32[]{:S(2)}) collective-permute-start(f32[16]{0:T(128)S(1)} %get-tuple-element.17), channel_id=1, source_target_pairs={{0,16},{8,24},{16,32},{24,40},{32,48},{40,56},{48,64},{56,72},{64,... | collective-permute-start | bytes 200 | tf_op jit(solution)/shard_map/ppermute | solution.py:16
  160.0 10.6 %collective-permute-start.9 = (bf16[16,16384]{1,0:T(8,128)(2,1)S(1)}, bf16[16,16384]{1,0:T(8,128)(2,1)S(1)}, u32[]{:S(2)}, u32[]{:S(2)}) collective-permute-start(bf16[16,16384]{1,0:T(8,128)(2,1)S(1)} %fusion.32), channel_id=1, source_target_pairs={{0,64},{8,72},{16,80},{24,88},{32,96},{40,104},{48,112},{56,120},{... | collective-permute-start | bytes 1572872 | tf_op jit(solution)/shard_map/ppermute | solution.py:17
  161.5 9.0 %collective-permute-start.3 = (f32[16]{0:T(128)S(1)}, f32[16]{0:T(128)S(1)}, u32[]{:S(2)}, u32[]{:S(2)}) collective-permute-start(f32[16]{0:T(128)S(1)} %get-tuple-element.15), channel_id=1, source_target_pairs={{0,32},{8,40},{16,48},{24,56},{32,64},{40,72},{48,80},{56,88},{64,... | collective-permute-start | bytes 200 | tf_op jit(solution)/shard_map/ppermute | solution.py:16
  171.9 29.1 %collective-permute-start.10 = (bf16[16,16384]{1,0:T(8,128)(2,1)}, bf16[16,16384]{1,0:T(8,128)(2,1)}, u32[]{:S(2)}, u32[]{:S(2)}) collective-permute-start(bf16[16,16384]{1,0:T(8,128)(2,1)} %fusion.38), channel_id=1, source_target_pairs={{0,128},{8,136},{16,144},{24,152},{32,160},{40,168},{48,176},{56,1... | collective-permute-start | bytes 1572872 | tf_op jit(solution)/shard_map/ppermute | solution.py:17
  191.0 4.8 %copy-start.7 = (bf16[512,1,256]{2,0,1:T(8,128)(2,1)S(1)}, bf16[512,1,256]{2,0,1:T(8,128)(2,1)}, u32[]{:S(2)}) copy-start(bf16[512,1,256]{2,0,1:T(8,128)(2,1)} %param.14) | copy-start | bytes 786436
  196.9 4.1 %collective-permute-start.4 = (f32[16]{0:T(128)S(1)}, f32[16]{0:T(128)S(1)}, u32[]{:S(2)}, u32[]{:S(2)}) collective-permute-start(f32[16]{0:T(128)S(1)} %get-tuple-element.13), channel_id=1, source_target_pairs={{0,64},{8,72},{16,80},{24,88},{32,96},{40,104},{48,112},{56,120},{... | collective-permute-start | bytes 200 | tf_op jit(solution)/shard_map/ppermute | solution.py:16
  205.7 6.0 %copy-start.10 = (f32[2,256,16]{1,2,0:T(8,128)S(1)}, f32[2,256,16]{1,2,0:T(8,128)}, u32[]{:S(2)}) copy-start(f32[2,256,16]{1,2,0:T(8,128)} %get-tuple-element.21) | copy-start | bytes 98308
  205.7 6.0 %copy-start.14 = (f32[16]{0:T(128)S(1)}, f32[16]{0:T(128)}, u32[]{:S(2)}) copy-start(f32[16]{0:T(128)} %param.17) | copy-start | bytes 196
  206.3 5.4 %copy-start.3 = (f32[2,256,16,64]{1,3,2,0:T(8,128)S(1)}, f32[2,256,16,64]{1,3,2,0:T(8,128)}, u32[]{:S(2)}) copy-start(f32[2,256,16,64]{1,3,2,0:T(8,128)} %copy.44) | copy-start | bytes 6291460
  206.3 5.4 %copy-start.5 = (bf16[2,256,16,64]{1,3,2,0:T(8,128)(2,1)S(1)}, bf16[2,256,16,64]{1,3,2,0:T(8,128)(2,1)}, u32[]{:S(2)}) copy-start(bf16[2,256,16,64]{1,3,2,0:T(8,128)(2,1)} %copy-done.4) | copy-start | bytes 3145732
  206.3 5.4 %copy-start.8 = (f32[2,256,256]{2,1,0:T(8,128)S(1)}, f32[2,256,256]{2,1,0:T(8,128)}, u32[]{:S(2)}) copy-start(f32[2,256,256]{2,1,0:T(8,128)} %fusion.44) | copy-start | bytes 1572868
  214.8 1.9 copy-start.11
  216.4 8.8 %copy-start.6 = (f32[64,4096]{1,0:T(8,128)S(1)}, f32[64,4096]{1,0:T(8,128)}, u32[]{:S(2)}) copy-start(f32[64,4096]{1,0:T(8,128)} %convert_element_type.96) | copy-start | bytes 3145732
  234.9 0.7 copy-start.9
  343.3 4.6 %copy-start.2 = (bf16[512,4096]{1,0:T(8,128)(2,1)S(1)}, bf16[512,4096]{1,0:T(8,128)(2,1)}, u32[]{:S(2)}) copy-start(bf16[512,4096]{1,0:T(8,128)(2,1)} %all-reduce.3.cloned.1.call-done) | copy-start | bytes 12582916
  347.9 3.6 copy-start.12
  347.9 3.6 copy-start.13
  351.5 5.6 %copy-start.1 = (bf16[512,1,256]{2,0,1:T(8,128)(2,1)S(1)}, bf16[512,1,256]{2,0,1:T(8,128)(2,1)}, u32[]{:S(2)}) copy-start(bf16[512,1,256]{2,0,1:T(8,128)(2,1)} %param.15) | copy-start | bytes 786436
Sparse Core Ops, SparseCore 0:
  10.6 109.2 all-gather.2
  122.3 102.8 all-gather.4
  235.1 108.1 all-reduce.2
where the time goes:
time: 364 us
  waiting for transfers between devices  192 us (53%)
  starting transfers between devices  83.4 us (23%)
  matrix products  31 us (9%)
  local copies, waits for them, and re-layouts  26.1 us (7%)
  other arithmetic  16.6 us (5%)
  between operations  14.8 us (4%)
    psum x1, waiting for transfers between devices, body(): hidden = lax.psum(with_residual, 'head').astype(jnp.float32)  106 us
    ppermute x6, starting transfers between devices, shifted(): lax.ppermute(s.astype(jnp.bfloat16), axis, pairs).astype(jnp.float32)  63.3 us
    ppermute x5, waiting for transfers between devices, shifted(): lax.ppermute(a, axis, pairs)  47 us
    ppermute x6, waiting for transfers between devices, shifted(): lax.ppermute(s.astype(jnp.bfloat16), axis, pairs).astype(jnp.float32)  29.4 us
    ppermute x5, starting transfers between devices, shifted(): lax.ppermute(a, axis, pairs)  20 us
    dot_general x1, matrix products, body(): jnp.dot(ssd_out, lax.all_gather(w_out, 'seq', axis=1, tiled=True), prefer...  9.75 us
    convert_element_type x2, local copies, waits for them, and re-layouts, body(): gate_z.reshape(block_count, SPAN, head_count, head_width)  8.7 us
    all_gather x1, waiting for transfers between devices, body(): lax.all_gather(w_out, 'seq', axis=1, tiled=True)  8.23 us
  transfers between devices with their start and end apart: 14, of which 9 were waited for; matrix products, arithmetic and copies ran while one was open for 14% of the time, Pallas kernels for 0%

commit v1 on v0

--- a/solution.py
+++ b/solution.py
@@ -120,7 +120,7 @@
         preferred_element_type=jnp.float32,
     )
     with_residual = (partial_sum + residual_rows).astype(jnp.bfloat16)
-    hidden = lax.psum(with_residual, "head").astype(jnp.float32)
+    hidden = jnp.sum(lax.all_gather(with_residual, "head"), axis=0).astype(jnp.float32)
     unit = refusal / jnp.sqrt(jnp.sum(refusal * refusal) + 1e-06)
     coef = jnp.dot(hidden, unit, precision=lax.Precision.HIGH)
     stream_all = (hidden - coef[:, None] * unit[None, :]).astype(jnp.bfloat16)

time: 364 us -> 602 us (1.65)
  waiting for transfers between devices: 192 us -> 385 us
  starting transfers between devices: 83.4 us -> 114 us
  other arithmetic: 16.6 us -> 29.8 us
    all_gather x0 -> x1, waiting for transfers between devices: none -> 326 us  [body(): lax.all_gather(with_residual, 'head')]
    psum x1 -> x0, waiting for transfers between devices: 106 us -> none  [body(): hidden = lax.psum(with_residual, 'head').astype(jnp.float32)]
    ppermute x6, starting transfers between devices: 63.3 us -> 99.8 us  [shifted(): lax.ppermute(s.astype(jnp.bfloat16), axis, pairs).astype(jnp.float32)]
    ppermute x5, waiting for transfers between devices: 47 us -> 21.7 us  [shifted(): lax.ppermute(a, axis, pairs)]
    reduce_sum x0 -> x1, other arithmetic: none -> 14 us  [body(): jnp.sum(lax.all_gather(with_residual, 'head'), axis=0).astype(jnp.float32)]
  transfers between devices with their start and end apart: 14 -> 14, of which waited for: 9 -> 9; matrix products, arithmetic and copies ran while one was open for 14% -> 8% of each run, Pallas kernels for 0% -> 0%
where the time goes in v1:
time: 602 us; the launch traced here: 601 us
  waiting for transfers between devices  385 us (64%)
  starting transfers between devices  114 us (19%)
  matrix products  33.6 us (6%)
  other arithmetic  29.8 us (5%)
  local copies, waits for them, and re-layouts  24 us (4%)
  between operations  14.8 us (2%)
    all_gather x1, waiting for transfers between devices, body(): lax.all_gather(with_residual, 'head')  326 us
    ppermute x6, starting transfers between devices, shifted(): lax.ppermute(s.astype(jnp.bfloat16), axis, pairs).astype(jnp.float32)  99.8 us
    ppermute x6, waiting for transfers between devices, shifted(): lax.ppermute(s.astype(jnp.bfloat16), axis, pairs).astype(jnp.float32)  25.1 us
    ppermute x5, waiting for transfers between devices, shifted(): lax.ppermute(a, axis, pairs)  21.7 us
    ppermute x5, starting transfers between devices, shifted(): lax.ppermute(a, axis, pairs)  14.3 us
    reduce_sum x1, other arithmetic, body(): jnp.sum(lax.all_gather(with_residual, 'head'), axis=0).astype(jnp.float32)  14 us
  transfers between devices with their start and end apart: 14, of which 9 were waited for; matrix products, arithmetic and copies ran while one was open for 8% of the time, Pallas kernels for 0%

profile of v1, /device:TPU:1, one launch (start us, length us, event | category | flops | bytes accessed | tf_op | source)
XLA Modules:
  0.0 601.5 jit_solution(6095658802147858071)
XLA Ops:
  8.0 0.8 copy_bitcast_fusion.1
  8.7 1.1 reduce-window.6
  10.1 3.0 reshape.188
  13.0 1.7 copy.36
  14.7 1.2 convert_element_type.81
  16.4 0.7 exponential_bitcast_fusion
  17.1 1.6 fusion.6
  18.7 1.6 fusion.43
  21.6 1.8 copy.38
  23.4 1.6 squeeze.4
  25.0 1.4 add_convert_fusion
  26.4 6.3 %collective-permute-start.5 = (bf16[16,16384]{1,0:T(8,128)(2,1)S(1)}, bf16[16,16384]{1,0:T(8,128)(2,1)S(1)}, u32[]{:S(2)}, u32[]{:S(2)}) collective-permute-start(bf16[16,16384]{1,0:T(8,128)(2,1)S(1)} %add_convert_fusion), channel_id=1, source_target_pairs={{0,8},{8,16},{16,24},{24,32},{32,40},{40,48},{48,56},{56,64},{64,7... | collective-permute-start | bytes 1572872 | tf_op jit(solution)/shard_map/ppermute | solution.py:17
  32.8 15.2 %collective-permute-done.5 = bf16[16,16384]{1,0:T(8,128)(2,1)S(1)} collective-permute-done((bf16[16,16384]{1,0:T(8,128)(2,1)S(1)}, bf16[16,16384]{1,0:T(8,128)(2,1)S(1)}, u32[]{:S(2)}, u32[]{:S(2)}) %collective-permute-start.5) | collective-permute-done | bytes 524320 | tf_op jit(solution)/shard_map/ppermute | solution.py:17
  47.9 5.3 collective-permute-start.6
  53.2 3.9 collective-permute-start
  57.1 8.2 %collective-permute-done = f32[16]{0:T(128)S(1)} collective-permute-done((f32[16]{0:T(128)S(1)}, f32[16]{0:T(128)S(1)}, u32[]{:S(2)}, u32[]{:S(2)}) %collective-permute-start) | collective-permute-done | bytes 96 | tf_op jit(solution)/shard_map/ppermute | solution.py:16
  65.3 6.0 collective-permute-start.1
  71.3 0.7 collective-permute-done.1
  72.3 47.0 %collective-permute-start.7 = (bf16[16,16384]{1,0:T(8,128)(2,1)S(1)}, bf16[16,16384]{1,0:T(8,128)(2,1)S(1)}, u32[]{:S(2)}, u32[]{:S(2)}) collective-permute-start(bf16[16,16384]{1,0:T(8,128)(2,1)S(1)} %fusion.31), channel_id=1, source_target_pairs={{0,16},{8,24},{16,32},{24,40},{32,48},{40,56},{48,64},{56,72},{64,... | collective-permute-start | bytes 1572872 | tf_op jit(solution)/shard_map/ppermute | solution.py:17
  119.4 6.0 collective-permute-done.7
  125.7 6.6 %collective-permute-start.8 = (bf16[16,16384]{1,0:T(8,128)(2,1)S(1)}, bf16[16,16384]{1,0:T(8,128)(2,1)S(1)}, u32[]{:S(2)}, u32[]{:S(2)}) collective-permute-start(bf16[16,16384]{1,0:T(8,128)(2,1)S(1)} %fusion.39), channel_id=1, source_target_pairs={{0,32},{8,40},{16,48},{24,56},{32,64},{40,72},{48,80},{56,88},{64,... | collective-permute-start | bytes 1572872 | tf_op jit(solution)/shard_map/ppermute | solution.py:17
  132.3 1.3 collective-permute-start.2
  133.6 12.1 %collective-permute-done.2 = f32[16]{0:T(128)S(1)} collective-permute-done((f32[16]{0:T(128)S(1)}, f32[16]{0:T(128)S(1)}, u32[]{:S(2)}, u32[]{:S(2)}) %collective-permute-start.2) | collective-permute-done | bytes 96 | tf_op jit(solution)/shard_map/ppermute | solution.py:16
  146.2 17.2 %collective-permute-start.9 = (bf16[16,16384]{1,0:T(8,128)(2,1)S(1)}, bf16[16,16384]{1,0:T(8,128)(2,1)S(1)}, u32[]{:S(2)}, u32[]{:S(2)}) collective-permute-start(bf16[16,16384]{1,0:T(8,128)(2,1)S(1)} %fusion.32), channel_id=1, source_target_pairs={{0,64},{8,72},{16,80},{24,88},{32,96},{40,104},{48,112},{56,120},{... | collective-permute-start | bytes 1572872 | tf_op jit(solution)/shard_map/ppermute | solution.py:17
  163.4 1.4 collective-permute-start.3
  164.8 0.7 collective-permute-done.3
  165.5 3.9 collective-permute-done.9
  169.4 1.3 fusion.38
  170.7 17.4 %collective-permute-start.10 = (bf16[16,16384]{1,0:T(8,128)(2,1)}, bf16[16,16384]{1,0:T(8,128)(2,1)}, u32[]{:S(2)}, u32[]{:S(2)}) collective-permute-start(bf16[16,16384]{1,0:T(8,128)(2,1)} %fusion.38), channel_id=1, source_target_pairs={{0,128},{8,136},{16,144},{24,152},{32,160},{40,168},{48,176},{56,1... | collective-permute-start | bytes 1572872 | tf_op jit(solution)/shard_map/ppermute | solution.py:17
  188.1 4.1 reshape.189
  192.3 4.6 copy.44
  197.0 1.1 fusion.44
  198.1 1.8 collective-permute-start.4
  199.8 2.2 convert_element_type.98
  202.0 1.8 multiply_add_fusion
  203.9 0.8 mul.195
  205.3 5.3 fusion.21
  210.7 3.1 multiply_reduce_fusion
  213.8 1.6 copy.45
  215.9 11.3 %all-gather.7.cloned.1.call-done = bf16[1024,4096]{1,0:T(8,128)(2,1)} async-done(((bf16[1024,128]{1,0:T(8,128)(2,1)}), bf16[1024,4096]{1,0:T(8,128)(2,1)}) %all-gather.7.cloned.1.call-update) | async-done | bytes 8388624 | tf_op jit(solution)/shard_map/all_gather | solution.py:119
  227.2 9.7 %fusion.4 = bf16[512,4096]{1,0:T(8,128)(2,1)} fusion(bf16[512,1024]{0,1:T(8,128)(2,1)S(1)} %multiply_convert_fusion.4, bf16[1024,4096]{1,0:T(8,128)(2,1)} %all-gather.7.cloned.1.call-done, f32[64,4096]{1,0:T(8,128)S(1)} %copy-done.7, pred[512]{0:T(512)(128)(4,1)S(1)} %broadcast_in_dim.63), kind=kOutput, calls=%fused_computation.7 | convolution fusion | flops 4301258752 | bytes 14680576 | tf_op jit(solution)/shard_map/dot_general | solution.py:117
  237.0 0.7 copy-done.10
  239.0 326.3 %all-gather.9.cloned.1.call-done = bf16[4096,4096]{1,0:T(8,128)(2,1)} async-done(((bf16[512,4096]{1,0:T(8,128)(2,1)}), bf16[4096,4096]{1,0:T(8,128)(2,1)}) %all-gather.9.cloned.1.call-update) | async-done | bytes 33554448 | tf_op jit(solution)/shard_map/all_gather | solution.py:123
  565.3 14.0 %reduce_sum.50 = bf16[512,4096]{1,0:T(8,128)(2,1)} reduce(bf16[8,512,4096]{2,1,0:T(8,128)(2,1)} %bitcast.68, bf16[]{:T(256)} %constant.10.clone.1), dimensions={0}, to_apply=%region_5.6 | reduce | flops 14680064 | bytes 37748736 | tf_op jit(solution)/shard_map/reduce_sum | solution.py:123
  579.4 4.6 fusion.45
  584.0 1.9 fusion
  585.9 0.8 constant_dynamic-slice_fusion
  586.8 8.2 %fusion.26 = bf16[512,1024]{1,0:T(8,128)(2,1)} fusion(bf16[4096,1024]{1,0:T(8,128)(2,1)} %all-gather.5.cloned.1.call-done, bf16[512,4096]{1,0:T(8,128)(2,1)S(1)} %get-tuple-element.11, f32[4096]{0:T(1024)S(1)} %copy-done.13, f32[512]{0:T(512)S(1)} %add_rsqrt_fusion), kind=kOutput, calls=%fused_computation.34 | convolution fusion | flops 4303880192 | bytes 13649920 | tf_op jit(solution)/shard_map/dot_general | solution.py:134
  (69 shorter events, 5.7 us)
Async XLA Ops:
  7.2 189.8 %copy-start = (bf16[512,1,256]{2,0,1:T(8,128)(2,1)S(1)}, bf16[512,1,256]{2,0,1:T(8,128)(2,1)}, u32[]{:S(2)}) copy-start(bf16[512,1,256]{2,0,1:T(8,128)(2,1)} %param.15) | copy-start | bytes 786436
  7.2 208.8 %all-gather.5.cloned.1.call-start = ((), (), s32[]{:S(2)}) async-start(), calls=%async_computation | async-start | bytes 8650752 | tf_op jit(solution)/shard_map/all_gather | solution.py:108
  7.9 219.3 %all-gather.7.cloned.1.call-start = ((), (), s32[]{:S(2)}) async-start(), calls=%async_computation.1 | async-start | bytes 8650752 | tf_op jit(solution)/shard_map/all_gather | solution.py:119
  14.7 5.6 copy-start.5
  26.4 21.5 %collective-permute-start.5 = (bf16[16,16384]{1,0:T(8,128)(2,1)S(1)}, bf16[16,16384]{1,0:T(8,128)(2,1)S(1)}, u32[]{:S(2)}, u32[]{:S(2)}) collective-permute-start(bf16[16,16384]{1,0:T(8,128)(2,1)S(1)} %add_convert_fusion), channel_id=1, source_target_pairs={{0,8},{8,16},{16,24},{24,32},{32,40},{40,48},{48,56},{56,64},{64,7... | collective-permute-start | bytes 1572872 | tf_op jit(solution)/shard_map/ppermute | solution.py:17
  47.9 24.1 %collective-permute-start.6 = (bf16[16,16384]{1,0:T(8,128)(2,1)S(1)}, bf16[16,16384]{1,0:T(8,128)(2,1)S(1)}, u32[]{:S(2)}, u32[]{:S(2)}) collective-permute-start(bf16[16,16384]{1,0:T(8,128)(2,1)S(1)} %collective-permute-done.5), channel_id=1, source_target_pairs={{0,8},{8,16},{16,24},{24,32},{32,40},{40,48},{48,56},{56,64},{64,7... | collective-permute-start | bytes 1572872 | tf_op jit(solution)/shard_map/ppermute | solution.py:17
  53.2 12.1 %collective-permute-start = (f32[16]{0:T(128)S(1)}, f32[16]{0:T(128)S(1)}, u32[]{:S(2)}, u32[]{:S(2)}) collective-permute-start(f32[16]{0:T(128)S(1)} %get-tuple-element.6), channel_id=1, source_target_pairs={{0,8},{8,16},{16,24},{24,32},{32,40},{40,48},{48,56},{56,64},{64,7... | collective-permute-start | bytes 200 | tf_op jit(solution)/shard_map/ppermute | solution.py:16
  65.3 6.7 %collective-permute-start.1 = (f32[16]{0:T(128)S(1)}, f32[16]{0:T(128)S(1)}, u32[]{:S(2)}, u32[]{:S(2)}) collective-permute-start(f32[16]{0:T(128)S(1)} %collective-permute-done), channel_id=1, source_target_pairs={{0,8},{8,16},{16,24},{24,32},{32,40},{40,48},{48,56},{56,64},{64,7... | collective-permute-start | bytes 200 | tf_op jit(solution)/shard_map/ppermute | solution.py:16
  72.3 53.1 %collective-permute-start.7 = (bf16[16,16384]{1,0:T(8,128)(2,1)S(1)}, bf16[16,16384]{1,0:T(8,128)(2,1)S(1)}, u32[]{:S(2)}, u32[]{:S(2)}) collective-permute-start(bf16[16,16384]{1,0:T(8,128)(2,1)S(1)} %fusion.31), channel_id=1, source_target_pairs={{0,16},{8,24},{16,32},{24,40},{32,48},{40,56},{48,64},{56,72},{64,... | collective-permute-start | bytes 1572872 | tf_op jit(solution)/shard_map/ppermute | solution.py:17
  119.3 446.0 %all-gather.9.cloned.1.call-start = ((), (), s32[]{:S(2)}) async-start(), calls=%async_computation.2 | async-start | bytes 37748736 | tf_op jit(solution)/shard_map/all_gather | solution.py:123
  125.7 20.0 %collective-permute-start.8 = (bf16[16,16384]{1,0:T(8,128)(2,1)S(1)}, bf16[16,16384]{1,0:T(8,128)(2,1)S(1)}, u32[]{:S(2)}, u32[]{:S(2)}) collective-permute-start(bf16[16,16384]{1,0:T(8,128)(2,1)S(1)} %fusion.39), channel_id=1, source_target_pairs={{0,32},{8,40},{16,48},{24,56},{32,64},{40,72},{48,80},{56,88},{64,... | collective-permute-start | bytes 1572872 | tf_op jit(solution)/shard_map/ppermute | solution.py:17
  132.3 13.4 %collective-permute-start.2 = (f32[16]{0:T(128)S(1)}, f32[16]{0:T(128)S(1)}, u32[]{:S(2)}, u32[]{:S(2)}) collective-permute-start(f32[16]{0:T(128)S(1)} %get-tuple-element.17), channel_id=1, source_target_pairs={{0,16},{8,24},{16,32},{24,40},{32,48},{40,56},{48,64},{56,72},{64,... | collective-permute-start | bytes 200 | tf_op jit(solution)/shard_map/ppermute | solution.py:16
  146.2 23.3 %collective-permute-start.9 = (bf16[16,16384]{1,0:T(8,128)(2,1)S(1)}, bf16[16,16384]{1,0:T(8,128)(2,1)S(1)}, u32[]{:S(2)}, u32[]{:S(2)}) collective-permute-start(bf16[16,16384]{1,0:T(8,128)(2,1)S(1)} %fusion.32), channel_id=1, source_target_pairs={{0,64},{8,72},{16,80},{24,88},{32,96},{40,104},{48,112},{56,120},{... | collective-permute-start | bytes 1572872 | tf_op jit(solution)/shard_map/ppermute | solution.py:17
  163.4 2.1 collective-permute-start.3
  169.4 22.8 %copy-start.4 = (bf16[16,16384]{1,0:T(8,128)(2,1)}, bf16[16,16384]{1,0:T(8,128)(2,1)S(1)}, u32[]{:S(2)}) copy-start(bf16[16,16384]{1,0:T(8,128)(2,1)S(1)} %collective-permute-done.9) | copy-start | bytes 1572868
  170.7 31.3 %collective-permute-start.10 = (bf16[16,16384]{1,0:T(8,128)(2,1)}, bf16[16,16384]{1,0:T(8,128)(2,1)}, u32[]{:S(2)}, u32[]{:S(2)}) collective-permute-start(bf16[16,16384]{1,0:T(8,128)(2,1)} %fusion.38), channel_id=1, source_target_pairs={{0,128},{8,136},{16,144},{24,152},{32,160},{40,168},{48,176},{56,1... | collective-permute-start | bytes 1572872 | tf_op jit(solution)/shard_map/ppermute | solution.py:17
  192.3 4.8 copy-start.8
  198.1 3.9 collective-permute-start.4
  204.7 6.0 copy-start.11
  204.7 6.0 copy-start.14
  205.3 5.4 copy-start.3
  205.3 5.4 copy-start.6
  205.3 5.4 copy-start.9
  213.8 1.9 copy-start.12
  215.4 11.8 %copy-start.7 = (f32[64,4096]{1,0:T(8,128)S(1)}, f32[64,4096]{1,0:T(8,128)}, u32[]{:S(2)}) copy-start(f32[64,4096]{1,0:T(8,128)} %convert_element_type.98) | copy-start | bytes 3145732
  237.0 0.7 copy-start.10
  579.4 4.6 copy-start.2
  584.0 2.8 copy-start.13
  586.8 8.2 %copy-start.1 = (bf16[512,1,256]{2,0,1:T(8,128)(2,1)S(1)}, bf16[512,1,256]{2,0,1:T(8,128)(2,1)}, u32[]{:S(2)}) copy-start(bf16[512,1,256]{2,0,1:T(8,128)(2,1)} %param.15) | copy-start | bytes 786436
Sparse Core Ops, SparseCore 0:
  10.6 109.2 all-gather.4
  122.3 104.8 all-gather.6
  237.1 328.1 all-gather.8
